TPU v7x, 32 devices: a whole 2x2x4 slice. The times are simulated.
32 devices in a mesh: img: 4 (over z), ref: 8 (over y, x, core).
Axes of the slice: x: 2, y: 2, z: 4, core: 2. Of those that a mesh axis runs over, the one named last changes fastest.
Arguments:
- images: bfloat16 [2048, 9216], P(('img', 'ref')), may hold values from -96 to 96
- references: bfloat16 [6912, 9216], P('ref'), may hold values from -0.5 to 0.5
- class_prior: float32 [192], P('ref'), may hold values from 0.2 to 5
Outputs:
- class_sums: float32 [192, 9216], P('ref', 'img')
- class_weights: float32 [192], P('ref')
All inputs are finite; a program needn't handle non-finite values.
Results may differ from a plain program's by a relative error of at most 0.0021.
Values may be sent and summed in bfloat16 or wider, within the bound.
No kernel may reach another device: no remote copies, remote signals or barrier semaphores. Data moves between devices by JAX's collectives and lax.ppermute only.
A program may use at most 128 MiB of HBM per device.

v0:
```python
import jax
import jax.numpy as jnp
from jax import lax
from jax.sharding import PartitionSpec as P

ANG = 144


def unturn(stacked, shift_size):
    classes_here, rotations, columns = stacked.shape
    cycles = stacked.reshape(classes_here, rotations, columns // ANG, ANG)
    doubled = jnp.concatenate([cycles, cycles], axis=3)
    result = doubled[:, 0, :, 0:ANG]
    for turn_index in range(1, rotations):
        start_col = turn_index * shift_size
        result = result + doubled[:, turn_index, :, start_col : start_col + ANG]
    return result.reshape(classes_here, columns)


def per_device(images, references, class_prior):
    local_refs, pixels = references.shape
    classes_here = class_prior.shape[0]
    rotations = local_refs // classes_here
    shift_size = ANG // rotations
    half_norm = 0.5 * jnp.einsum(
        "jp,jp->j", references, references, preferred_element_type=jnp.float32
    )
    offsets = (jnp.log(class_prior)[:, None] - half_norm.reshape(classes_here, rotations)).reshape(
        local_refs
    )
    gathered = lax.all_gather(images, "ref", axis=0, tiled=True)
    products = lax.dot_general(
        gathered, references, (((1,), (1,)), ((), ())), preferred_element_type=jnp.float32
    )
    scores = products + offsets
    local_max = jnp.max(scores, axis=1)
    top_score = lax.pmax(local_max, "ref")
    denominator = lax.psum(jnp.sum(jnp.exp(scores - top_score[:, None]), axis=1), "ref")
    weights = (jnp.exp(scores - top_score[:, None]) / denominator[:, None]).astype(jnp.bfloat16)
    local_mass = (
        jnp.sum(weights.astype(jnp.float32), axis=0).reshape(classes_here, rotations).sum(axis=1)
    )
    class_weights = lax.psum(local_mass, "img")
    sums = lax.dot_general(
        weights, gathered, (((0,), (0,)), ((), ())), preferred_element_type=jnp.float32
    )
    reduced = lax.psum_scatter(sums, "img", scatter_dimension=1, tiled=True)
    class_sums = unturn(reduced.reshape(classes_here, rotations, -1), shift_size)
    return (class_sums, class_weights)


def solution(mesh):
    placed = (P(("img", "ref"), None), P("ref", None), P("ref"))
    return jax.shard_map(
        per_device,
        mesh=mesh,
        in_specs=placed,
        out_specs=(P("ref", "img"), P("ref")),
        check_vma=False,
    )
```

profile of v0, /device:TPU:0, one launch (start us, length us, event | category | flops | bytes accessed | tf_op | source)
XLA Modules:
  0.0 719.0 jit_solution(10911316544609606139)
XLA Ops:
  8.8 7.0 fusion
  15.8 55.7 %all-gather.2.cloned.1.call-done = bf16[512,9216]{1,0:T(8,128)(2,1)} async-done(((bf16[64,9216]{1,0:T(8,128)(2,1)}), bf16[512,9216]{1,0:T(8,128)(2,1)}) %all-gather.2.cloned.1.call-update) | async-done | bytes 9437200 | tf_op jit(solution)/shard_map/all_gather | solution.py:31
  71.4 14.2 %add_reduce_fusion = (f32[512]{0:T(512)S(1)}, f32[512,864]{0,1:T(8,128)S(1)}) fusion(f32[864]{0:T(1024)S(1)} %multiply_subtract_fusion, bf16[512,9216]{1,0:T(8,128)(2,1)} %all-gather.2.cloned.1.call-done, bf16[864,9216]{1,0:T(8,128)(2,1)} %param.4), kind=kOutput, calls=%fused_computation.5 | convolution fusion | flops 8154611200 | bytes 27137408 | tf_op jit(solution)/shard_map/dot_general | solution.py:32
  85.6 13.1 %pmax.7 = f32[512]{0:T(512)S(1)} all-reduce(f32[512]{0:T(512)S(1)} %get-tuple-element.22), channel_id=1, replica_groups=mesh['img'=4,'ref'=8] {'ref'}, use_global_device_ids=true, to_apply=%region_1.0 | all-reduce | flops 512 | bytes 4096 | tf_op jit(solution)/shard_map/pmax | solution.py:37
  99.1 11.8 %psum.14 = f32[512]{0:T(512)S(1)} all-reduce(f32[512]{0:T(512)S(1)} %fusion.1), channel_id=1, replica_groups=mesh['img'=4,'ref'=8] {'ref'}, use_global_device_ids=true, to_apply=%region_3.0 | all-reduce | flops 512 | bytes 4096 | tf_op jit(solution)/shard_map/psum | solution.py:38
  111.4 17.6 %fusion.2 = f32[864,9216]{1,0:T(8,128)} fusion(bf16[512,864]{0,1:T(8,128)(2,1)S(1)} %get-tuple-element.3, bf16[512,9216]{1,0:T(8,128)(2,1)} %all-gather.2.cloned.1.call-done), kind=kOutput, calls=%fused_computation.44 | convolution fusion | flops 8153726976 | bytes 42172416 | tf_op jit(solution)/shard_map/dot_general | solution.py:44
  129.2 12.4 %psum.15 = f32[24]{0:T(128)} all-reduce(f32[24]{0:T(128)S(1)} %reduce_sum.29), channel_id=1, replica_groups=mesh['img'=4,'ref'=8] {'img'}, use_global_device_ids=true, to_apply=%region_7.0 | all-reduce | flops 24 | bytes 192 | tf_op jit(solution)/shard_map/psum | solution.py:43
  141.6 513.8 %reduce-scatter.2.cloned.1.call-done = f32[864,2304]{1,0:T(8,128)} async-done(((f32[864,9216]{1,0:T(8,128)}), f32[864,2304]{1,0:T(8,128)}) %reduce-scatter.2.cloned.1.call-update) | async-done | bytes 7962640 | tf_op jit(solution)/shard_map/reduce_scatter | solution.py:47
  655.4 15.2 %reshape_reshape.3 = f32[24,36,16,144]{3,2,1,0:T(8,128)} reshape(f32[864,2304]{1,0:T(8,128)} %reduce-scatter.2.cloned.1.call-done) | data formatting | bytes 15925248 | tf_op jit(solution)/shard_map/reshape;reshape | solution.py:11
  670.6 8.5 %maximum_add_fusion = f32[24,1,16,144]{3,2,1,0:T(8,128)} fusion(f32[24,36,16,144]{3,2,1,0:T(8,128)} %reshape_reshape.3), kind=kLoop, calls=%fused_computation.26 | loop fusion | flops 1769472 | bytes 14770176 | tf_op jit(solution)/shard_map/add | solution.py:16
  680.2 3.5 pad_maximum_fusion.18
  683.7 2.5 pad_maximum_fusion.17
  686.2 1.9 reshape.71
  688.1 1.9 squeeze.128
  690.0 1.9 squeeze.111
  691.9 1.9 squeeze.110
  693.8 1.9 squeeze.126
  695.6 1.9 squeeze.118
  697.5 1.9 squeeze.122
  699.4 1.9 squeeze.117
  701.3 1.9 squeeze.124
  703.2 1.9 squeeze.116
  705.1 1.9 squeeze.121
  709.5 2.7 add_add_fusion
  (24 shorter events, 6.4 us)
Async XLA Ops:
  7.2 64.3 %all-gather.2.cloned.1.call-start = ((), (), s32[]{:S(2)}) async-start(), calls=%async_computation.1 | async-start | bytes 10616832 | tf_op jit(solution)/shard_map/all_gather | solution.py:31
  7.9 647.5 %reduce-scatter.2.cloned.1.call-start = ((), (), s32[]{:S(2)}) async-start(), calls=%async_computation.2 | async-start | bytes 39813120 | tf_op jit(solution)/shard_map/reduce_scatter | solution.py:47
  670.6 8.6 %copy-start = (f32[24,36,16,144]{3,2,1,0:T(8,128)S(1)}, f32[24,36,16,144]{3,2,1,0:T(8,128)}, u32[]{:S(2)}) copy-start(f32[24,36,16,144]{3,2,1,0:T(8,128)} %reshape_reshape.3) | copy-start | bytes 23887876
Sparse Core Ops, SparseCore 0:
  9.9 61.5 all-gather.1
  129.1 526.1 reduce-scatter.1
where the time goes:
time: 720 us; the launch traced here: 719 us
  waiting for transfers between devices  570 us (79%)
  local copies, waits for them, and re-layouts  39.7 us (6%)
  blocking collectives  37.3 us (5%)
  matrix products  31.7 us (4%)
  other arithmetic  26.1 us (4%)
  between operations  14.1 us (2%)
    reduce_scatter x1, waiting for transfers between devices, per_device(): reduced = lax.psum_scatter(sums, 'img', scatter_dimension=1, tiled=True)  514 us
    all_gather x1, waiting for transfers between devices, per_device(): gathered = lax.all_gather(images, 'ref', axis=0, tiled=True)  55.7 us
    squeeze x19, local copies, waits for them, and re-layouts, unturn(): result = result + doubled[:, turn_index, :, start_col:start_col + ANG]  21.4 us
    dot_general x1, matrix products, per_device(): lax.dot_general(weights, gathered, (((0,), (0,)), ((), ())), preferred_el...  17.6 us
    another operation x1, local copies, waits for them, and re-layouts, unturn(): cycles = stacked.reshape(classes_here, rotations, columns // ANG, ANG)  15.2 us
  transfers between devices with their start and end apart: 2, of which 2 were waited for; matrix products, arithmetic and copies ran while one was open for 1% of the time, Pallas kernels for 0%

commit v1 on v0

--- a/solution.py
+++ b/solution.py
@@ -4,6 +4,18 @@
 from jax.sharding import PartitionSpec as P
 
 ANG = 144
+
+
+def doubled_up(shard, axis, dim):
+    ways, here, turn = (lax.axis_size(axis), lax.axis_index(axis), shard.shape[dim])
+    line, have = (shard, 1)
+    while have < ways:
+        line = jnp.concatenate(
+            [line, lax.ppermute(line, axis, [(d, (d - have) % ways) for d in range(ways)])],
+            axis=dim,
+        )
+        have = 2 * have
+    return jnp.roll(line, here * turn, axis=dim)
 
 
 def unturn(stacked, shift_size):
@@ -28,7 +40,7 @@
     offsets = (jnp.log(class_prior)[:, None] - half_norm.reshape(classes_here, rotations)).reshape(
         local_refs
     )
-    gathered = lax.all_gather(images, "ref", axis=0, tiled=True)
+    gathered = doubled_up(images, "ref", 0)
     products = lax.dot_general(
         gathered, references, (((1,), (1,)), ((), ())), preferred_element_type=jnp.float32
     )

time: 720 us -> 850 us (1.18)
  waiting for transfers between devices: 570 us -> 672 us
  local copies, waits for them, and re-layouts: 39.7 us -> 56.4 us
    ppermute x0 -> x3, waiting for transfers between devices: none -> 159 us  [doubled_up(): lax.ppermute(line, axis, [(d, (d - have) % ways) for d in range(ways)])]
    all_gather x1 -> x0, waiting for transfers between devices: 55.7 us -> none  [per_device(): gathered = lax.all_gather(images, 'ref', axis=0, tiled=True)]
    unnamed x2 -> x25, local copies, waits for them, and re-layouts: 0.17 us -> 12.6 us
  transfers between devices with their start and end apart: 2 -> 4, of which waited for: 2 -> 4; matrix products, arithmetic and copies ran while one was open for 1% -> 1% of each run, Pallas kernels for 0% -> 0%
where the time goes in v1:
time: 850 us; the launch traced here: 849 us
  waiting for transfers between devices  672 us (79%)
  local copies, waits for them, and re-layouts  56.4 us (7%)
  blocking collectives  37.4 us (4%)
  other arithmetic  34.4 us (4%)
  matrix products  29.7 us (3%)
  between operations  14.1 us (2%)
    reduce_scatter x1, waiting for transfers between devices, per_device(): reduced = lax.psum_scatter(sums, 'img', scatter_dimension=1, tiled=True)  513 us
    ppermute x3, waiting for transfers between devices, doubled_up(): lax.ppermute(line, axis, [(d, (d - have) % ways) for d in range(ways)])  159 us
    squeeze x19, local copies, waits for them, and re-layouts, unturn(): result = result + doubled[:, turn_index, :, start_col:start_col + ANG]  21.4 us
    dot_general x1, matrix products, per_device(): lax.dot_general(weights, gathered, (((0,), (0,)), ((), ())), preferred_el...  17.7 us
  transfers between devices with their start and end apart: 4, of which 4 were waited for; matrix products, arithmetic and copies ran while one was open for 1% of the time, Pallas kernels for 0%

profile of v1, /device:TPU:0, one launch (start us, length us, event | category | flops | bytes accessed | tf_op | source)
XLA Modules:
  0.0 848.6 jit_solution(8967913834083940004)
XLA Ops:
  7.2 3.4 collective-permute-start
  10.6 14.0 %collective-permute-done = bf16[64,9216]{1,0:T(8,128)(2,1)S(1)} collective-permute-done((bf16[64,9216]{1,0:T(8,128)(2,1)}, bf16[64,9216]{1,0:T(8,128)(2,1)S(1)}, u32[]{:S(2)}, u32[]{:S(2)}) %collective-permute-start) | collective-permute-done | bytes 1179680 | tf_op jit(solution)/shard_map/ppermute | solution.py:14
  27.1 53.0 %collective-permute-done.1 = bf16[128,9216]{1,0:T(8,128)(2,1)S(1)} collective-permute-done((bf16[128,9216]{1,0:T(8,128)(2,1)S(1)}, bf16[128,9216]{1,0:T(8,128)(2,1)S(1)}, u32[]{:S(2)}, u32[]{:S(2)}) %collective-permute-start.1) | collective-permute-done | bytes 2359328 | tf_op jit(solution)/shard_map/ppermute | solution.py:14
  80.1 3.4 pad_maximum_fusion
  84.4 7.1 fusion
  95.4 91.8 %collective-permute-done.2 = bf16[256,9216]{1,0:T(8,128)(2,1)} collective-permute-done((bf16[256,9216]{1,0:T(8,128)(2,1)}, bf16[256,9216]{1,0:T(8,128)(2,1)}, u32[]{:S(2)}, u32[]{:S(2)}) %collective-permute-start.2) | collective-permute-done | bytes 4718624 | tf_op jit(solution)/shard_map/ppermute | solution.py:14
  187.2 4.8 constant_dynamic-update-slice_fusion.4
  195.8 4.9 constant_dynamic-update-slice_fusion
  200.7 12.0 %add_reduce_fusion = (f32[512]{0:T(512)S(1)}, f32[512,864]{0,1:T(8,128)}) fusion(f32[864]{0:T(1024)S(1)} %multiply_subtract_fusion, bf16[864,9216]{1,0:T(8,128)(2,1)S(1)} %bitcast.43, bf16[1024,9216]{1,0:T(8,128)(2,1)} %constant_dynamic-update-slice_fusion, s32[]{:T(128)S(6)} %select_n.14), kind=kOutput, calls=%fused_computation.11 | convolution fusion | flops 8154611200 | bytes 27137412 | tf_op jit(solution)/shard_map/dot_general | solution.py:44
  212.7 13.0 %pmax.7 = f32[512]{0:T(512)S(1)} all-reduce(f32[512]{0:T(512)S(1)} %get-tuple-element.22), channel_id=1, replica_groups=mesh['img'=4,'ref'=8] {'ref'}, use_global_device_ids=true, to_apply=%region_1.2 | all-reduce | flops 512 | bytes 4096 | tf_op jit(solution)/shard_map/pmax | solution.py:49
  227.5 11.8 %psum.14 = f32[512]{0:T(512)S(1)} all-reduce(f32[512]{0:T(512)S(1)} %fusion.5), channel_id=1, replica_groups=mesh['img'=4,'ref'=8] {'ref'}, use_global_device_ids=true, to_apply=%region_3.4 | all-reduce | flops 512 | bytes 4096 | tf_op jit(solution)/shard_map/psum | solution.py:50
  239.3 2.0 convert_reduce_fusion
  241.3 17.7 %fusion.1 = f32[864,9216]{1,0:T(8,128)} fusion(bf16[512,864]{0,1:T(8,128)(2,1)S(1)} %get-tuple-element.3, bf16[1024,9216]{1,0:T(8,128)(2,1)} %constant_dynamic-update-slice_fusion, s32[]{:T(128)S(6)} %select_n.14), kind=kOutput, calls=%fused_computation.2 | convolution fusion | flops 8153726976 | bytes 42172420 | tf_op jit(solution)/shard_map/dot_general | solution.py:56
  259.3 12.6 %psum.15 = f32[24]{0:T(128)} all-reduce(f32[24]{0:T(128)S(1)} %reduce_sum.29), channel_id=1, replica_groups=mesh['img'=4,'ref'=8] {'img'}, use_global_device_ids=true, to_apply=%region_7.8 | all-reduce | flops 24 | bytes 192 | tf_op jit(solution)/shard_map/psum | solution.py:55
  271.9 513.0 %reduce-scatter.2.cloned.1.call-done = f32[864,2304]{1,0:T(8,128)} async-done(((f32[864,9216]{1,0:T(8,128)}), f32[864,2304]{1,0:T(8,128)}) %reduce-scatter.2.cloned.1.call-update) | async-done | bytes 7962640 | tf_op jit(solution)/shard_map/reduce_scatter | solution.py:59
  784.9 15.2 %reshape_reshape.3 = f32[24,36,16,144]{3,2,1,0:T(8,128)} reshape(f32[864,2304]{1,0:T(8,128)} %reduce-scatter.2.cloned.1.call-done) | data formatting | bytes 15925248 | tf_op jit(solution)/shard_map/reshape;reshape | solution.py:23
  800.2 8.5 maximum_add_fusion
  809.8 3.5 pad_maximum_fusion.20
  813.2 2.5 pad_maximum_fusion.19
  815.7 1.9 reshape.71
  819.5 1.9 squeeze.111
  828.9 1.9 squeeze.117
  832.7 1.9 squeeze.116
  839.1 2.7 add_add_fusion
  (54 shorter events, 30.0 us)
Async XLA Ops:
  7.2 77.1 %copy-start.4 = (f32[24]{0:T(128)S(1)}, f32[24]{0:T(128)}, u32[]{:S(2)}) copy-start(f32[24]{0:T(128)} %param.5) | copy-start | bytes 292
  7.2 777.7 %reduce-scatter.2.cloned.1.call-start = ((), (), s32[]{:S(2)}) async-start(), calls=%async_computation.1 | async-start | bytes 39813120 | tf_op jit(solution)/shard_map/reduce_scatter | solution.py:59
  7.2 17.4 %collective-permute-start = (bf16[64,9216]{1,0:T(8,128)(2,1)}, bf16[64,9216]{1,0:T(8,128)(2,1)S(1)}, u32[]{:S(2)}, u32[]{:S(2)}) collective-permute-start(bf16[64,9216]{1,0:T(8,128)(2,1)} %param.3), channel_id=1, source_target_pairs={{0,7},{1,0},{2,1},{3,2},{4,3},{5,4},{6,5},{7,6},{8,15},{9,8},{10,9... | collective-permute-start | bytes 3538952 | tf_op jit(solution)/shard_map/ppermute | solution.py:14
  24.6 55.5 %copy-start.2 = (bf16[64,9216]{1,0:T(8,128)(2,1)}, bf16[64,9216]{1,0:T(8,128)(2,1)S(1)}, u32[]{:S(2)}) copy-start(bf16[64,9216]{1,0:T(8,128)(2,1)S(1)} %collective-permute-done) | copy-start | bytes 3538948
  26.5 53.6 %collective-permute-start.1 = (bf16[128,9216]{1,0:T(8,128)(2,1)S(1)}, bf16[128,9216]{1,0:T(8,128)(2,1)S(1)}, u32[]{:S(2)}, u32[]{:S(2)}) collective-permute-start(bf16[128,9216]{1,0:T(8,128)(2,1)S(1)} %pad_maximum_fusion.1), channel_id=1, source_target_pairs={{0,6},{1,7},{2,0},{3,1},{4,2},{5,3},{6,4},{7,5},{8,14},{9,15},{10,... | collective-permute-start | bytes 7077896 | tf_op jit(solution)/shard_map/ppermute | solution.py:14
  83.5 8.0 copy-start.1
  83.5 103.6 %collective-permute-start.2 = (bf16[256,9216]{1,0:T(8,128)(2,1)}, bf16[256,9216]{1,0:T(8,128)(2,1)}, u32[]{:S(2)}, u32[]{:S(2)}) collective-permute-start(bf16[256,9216]{1,0:T(8,128)(2,1)} %pad_maximum_fusion), channel_id=1, source_target_pairs={{0,4},{1,5},{2,6},{3,7},{4,0},{5,1},{6,2},{7,3},{8,12},{9,13},{10,... | collective-permute-start | bytes 14155784 | tf_op jit(solution)/shard_map/ppermute | solution.py:14
  84.4 8.3 copy-start.3
  93.8 106.8 %slice-start = ((s8[15925248]{0:T(1024)(128)(4,1)}), s8[4194304]{0:T(1024)(128)(4,1)S(1)}, s32[]{:S(2)}) async-start(s8[15925248]{0:T(1024)(128)(4,1)} %bitcast.42), calls=%async_computation.2 | async-start | bytes 8388608
  95.4 105.3 %slice-start.1 = ((s8[15925248]{0:T(1024)(128)(4,1)}), s8[4194304]{0:T(1024)(128)(4,1)S(1)}, s32[]{:S(2)}) async-start(s8[15925248]{0:T(1024)(128)(4,1)} %bitcast.42), calls=%async_computation.3 | async-start | bytes 8388608
  193.1 7.6 slice-start.2
  195.8 4.9 slice-start.3
  800.2 8.6 %copy-start = (f32[24,36,16,144]{3,2,1,0:T(8,128)S(1)}, f32[24,36,16,144]{3,2,1,0:T(8,128)}, u32[]{:S(2)}) copy-start(f32[24,36,16,144]{3,2,1,0:T(8,128)} %reshape_reshape.3) | copy-start | bytes 23887876
Sparse Core Ops, SparseCore 0:
  259.2 525.6 reduce-scatter.1
